TPU v7x, 32 devices: a whole 2x2x4 slice. The times are simulated.
32 devices in a mesh: shard: 8 (over z, x), tensor: 4 (over y, core).
Axes of the slice: x: 2, y: 2, z: 4, core: 2. Of those that a mesh axis runs over, the one named last changes fastest.
Arguments:
- wide_weight: bfloat16 [4, 4096, 4096], P(None, 'shard', 'tensor'), may hold values from -6 to 6
- wide_grad: bfloat16 [4, 4096, 4096], P(None, 'shard', 'tensor'), may hold values from -6 to 6
- wide_first: float32 [4, 4096, 256], P(None, ('shard', 'tensor')), may hold values from -4 to 4
- wide_second: float32 [4, 4096, 256], P(None, ('shard', 'tensor')), may hold values from 0.001 to 0.1
- wide_basis: bfloat16 [4, 4096, 256], P(None, 'tensor'), may hold values from -0.09375 to 0.09375
- narrow_weight: bfloat16 [4, 1024, 4096], P(None, 'shard', 'tensor'), may hold values from -6 to 6
- narrow_grad: bfloat16 [4, 1024, 4096], P(None, 'shard', 'tensor'), may hold values from -6 to 6
- narrow_first: float32 [4, 1024, 256], P(None, ('shard', 'tensor')), may hold values from -4 to 4
- narrow_second: float32 [4, 1024, 256], P(None, ('shard', 'tensor')), may hold values from 0.001 to 0.1
- narrow_basis: bfloat16 [4, 4096, 256], P(None, 'tensor'), may hold values from -0.09375 to 0.09375
- vocab_weight: bfloat16 [2, 32000, 4096], P(None, 'shard', 'tensor'), may hold values from -6 to 6
- vocab_grad: bfloat16 [2, 32000, 4096], P(None, 'shard', 'tensor'), may hold values from -6 to 6
- vocab_first: float32 [2, 32000, 256], P(None, ('shard', 'tensor')), may hold values from -4 to 4
- vocab_second: float32 [2, 32000, 256], P(None, ('shard', 'tensor')), may hold values from 0.001 to 0.1
- vocab_basis: bfloat16 [2, 4096, 256], P(None, 'tensor'), may hold values from -0.09375 to 0.09375
Outputs:
- wide_weight_new: bfloat16 [4, 4096, 4096], P(None, 'shard', 'tensor')
- wide_first_new: float32 [4, 4096, 256], P(None, ('shard', 'tensor'))
- wide_second_new: float32 [4, 4096, 256], P(None, ('shard', 'tensor'))
- narrow_weight_new: bfloat16 [4, 1024, 4096], P(None, 'shard', 'tensor')
- narrow_first_new: float32 [4, 1024, 256], P(None, ('shard', 'tensor'))
- narrow_second_new: float32 [4, 1024, 256], P(None, ('shard', 'tensor'))
- vocab_weight_new: bfloat16 [2, 32000, 4096], P(None, 'shard', 'tensor')
- vocab_first_new: float32 [2, 32000, 256], P(None, ('shard', 'tensor'))
- vocab_second_new: float32 [2, 32000, 256], P(None, ('shard', 'tensor'))
All inputs are finite; a program needn't handle non-finite values.
Results may differ from a plain program's by a relative error of at most 0.01.
Values may be sent and summed in bfloat16 or wider, within the bound.
No kernel may reach another device: no remote copies, remote signals or barrier semaphores. Data moves between devices by JAX's collectives and lax.ppermute only.
A program may use at most 192 MiB of HBM per device.

v0:
```python
import functools
import jax
import jax.numpy as jnp
from jax import lax
from jax.sharding import PartitionSpec as P

NS_ITERS = 3
HIGHEST = lax.Precision.HIGHEST


def local_gram(polish):
    return jnp.einsum("sdk,sdl->skl", polish, polish, precision=HIGHEST)


def polish_small(back, gram):
    trace = jnp.einsum("skk->s", gram)
    scale = 1.0 / jnp.sqrt(trace + 1e-06)
    small = gram * (scale * scale)[:, None, None]
    rank = gram.shape[1]
    eye = jnp.eye(rank, dtype=jnp.float32)[None, :, :]
    factor = jnp.broadcast_to(eye, gram.shape)
    for step in range(NS_ITERS):
        square = jnp.einsum("skl,slm->skm", small, small, precision=HIGHEST)
        turn = 3.4445 * eye - 4.775 * small + 2.0315 * square
        factor = jnp.einsum("skl,slm->skm", factor, turn, precision=HIGHEST)
        if step + 1 < NS_ITERS:
            small = jnp.einsum(
                "skl,slm->skm",
                turn,
                jnp.einsum("skl,slm->skm", small, turn, precision=HIGHEST),
                precision=HIGHEST,
            )
    return jnp.einsum("sdk,skl->sdl", back * scale[:, None, None], factor, precision=HIGHEST)


def adam_moments(first, second, projected):
    first_new = 0.9 * first + 0.1 * projected
    second_new = 0.999 * second + 0.001 * projected * projected
    direction = first_new / (1.0 - 0.9**10) / (jnp.sqrt(second_new / (1.0 - 0.999**10)) + 1e-08)
    return (first_new, second_new, direction.astype(jnp.bfloat16))


def split_rows(flat, shapes):
    parts = []
    offset = 0
    for shape in shapes:
        size = 1
        for dim in shape:
            size *= dim
        parts.append(flat[..., offset : offset + size].reshape(flat.shape[:-1] + shape))
        offset += size
    return parts


def per_device(
    tensor_size,
    wide_weight,
    wide_grad,
    wide_first,
    wide_second,
    wide_basis,
    narrow_weight,
    narrow_grad,
    narrow_first,
    narrow_second,
    narrow_basis,
    vocab_weight,
    vocab_grad,
    vocab_first,
    vocab_second,
    vocab_basis,
):
    weights = (wide_weight, narrow_weight, vocab_weight)
    grads = (wide_grad, narrow_grad, vocab_grad)
    firsts = (wide_first, narrow_first, vocab_first)
    seconds = (wide_second, narrow_second, vocab_second)
    olds = (wide_basis, narrow_basis, vocab_basis)
    counts = [grad.shape[0] for grad in grads]
    sketch_terms = [
        jnp.einsum("smc,scr->smr", grad, old, preferred_element_type=jnp.float32).astype(
            jnp.bfloat16
        )
        for grad, old in zip(grads, olds)
    ]
    sketches = lax.psum(tuple(sketch_terms), "tensor")
    back_terms = [
        jnp.einsum("smc,smr->scr", grad, sketch, preferred_element_type=jnp.float32)
        for grad, sketch in zip(grads, sketches)
    ]
    back_all = jnp.concatenate(back_terms, axis=0).astype(jnp.bfloat16)
    backs = lax.psum_scatter(back_all, "shard", scatter_dimension=1, tiled=True).astype(jnp.float32)
    grams = lax.psum(local_gram(backs), ("shard", "tensor"))
    rounded = polish_small(backs, grams).astype(jnp.bfloat16)
    basis_all = lax.all_gather(rounded, "shard", axis=1, tiled=True)
    bases = []
    offset = 0
    for count in counts:
        bases.append(basis_all[offset : offset + count])
        offset += count
    proj_parts = []
    row_shapes = []
    for grad, basis in zip(grads, bases):
        count, rows, cols = grad.shape
        split = grad.reshape(count, tensor_size, rows // tensor_size, cols)
        proj = jnp.einsum("sjmc,scr->jsmr", split, basis, preferred_element_type=jnp.float32)
        row_shapes.append((count, rows // tensor_size, basis.shape[2]))
        proj_parts.append(proj.reshape(tensor_size, -1, basis.shape[2]).astype(jnp.bfloat16))
    proj_all = jnp.concatenate(proj_parts, axis=1)
    proj_mine = lax.psum_scatter(proj_all, "tensor", scatter_dimension=0, tiled=True).reshape(-1)
    projected = [part.astype(jnp.float32) for part in split_rows(proj_mine, row_shapes)]
    results = [
        adam_moments(first, second, proj) for first, second, proj in zip(firsts, seconds, projected)
    ]
    dir_all = jnp.concatenate([result[2].reshape(-1) for result in results])
    dir_gathered = lax.all_gather(dir_all, "tensor", axis=0, tiled=False)
    directions = split_rows(dir_gathered, row_shapes)
    outputs = []
    for weight, direction, basis, result in zip(weights, directions, bases, results):
        count, rows, cols = weight.shape
        update = jnp.einsum("jsmr,scr->sjmc", direction, basis, preferred_element_type=jnp.float32)
        update = update.reshape(count, rows, cols)
        weight_new = (0.99 * weight.astype(jnp.float32) - 2.0 * update).astype(jnp.bfloat16)
        outputs.append((weight_new, result[0], result[1]))
    return (
        outputs[0][0],
        outputs[0][1],
        outputs[0][2],
        outputs[1][0],
        outputs[1][1],
        outputs[1][2],
        outputs[2][0],
        outputs[2][1],
        outputs[2][2],
    )


def solution(mesh):
    in_specs = (
        P(None, "shard", "tensor"),
        P(None, "shard", "tensor"),
        P(None, ("shard", "tensor"), None),
        P(None, ("shard", "tensor"), None),
        P(None, "tensor", None),
        P(None, "shard", "tensor"),
        P(None, "shard", "tensor"),
        P(None, ("shard", "tensor"), None),
        P(None, ("shard", "tensor"), None),
        P(None, "tensor", None),
        P(None, "shard", "tensor"),
        P(None, "shard", "tensor"),
        P(None, ("shard", "tensor"), None),
        P(None, ("shard", "tensor"), None),
        P(None, "tensor", None),
    )
    out_specs = (
        P(None, "shard", "tensor"),
        P(None, ("shard", "tensor"), None),
        P(None, ("shard", "tensor"), None),
        P(None, "shard", "tensor"),
        P(None, ("shard", "tensor"), None),
        P(None, ("shard", "tensor"), None),
        P(None, "shard", "tensor"),
        P(None, ("shard", "tensor"), None),
        P(None, ("shard", "tensor"), None),
    )
    return jax.shard_map(
        functools.partial(per_device, mesh.shape["tensor"]),
        mesh=mesh,
        in_specs=in_specs,
        out_specs=out_specs,
        check_vma=False,
    )
```

profile of v0, /device:TPU:0, one launch (start us, length us, event | category | flops | bytes accessed | tf_op | source)
XLA Modules:
  0.0 731.9 jit_solution(9271300986264332978)
XLA Ops:
  10.4 4.5 convolution_convert_fusion.2
  14.9 12.1 %convolution_convert_fusion = bf16[2,4000,256]{2,1,0:T(8,128)(2,1)} fusion(bf16[2,4000,1024]{2,1,0:T(8,128)(2,1)} %param.26, bf16[2,1024,256]{2,1,0:T(8,128)(2,1)S(1)} %copy-done.16), kind=kOutput, calls=%fused_computation.5 | convolution fusion | flops 4196352000 | bytes 21528576 | tf_op jit(solution)/shard_map/smc,scr->smr/dot_general | solution.py:80
  27.4 108.1 %all-reduce.6.cloned.1.call-done = (bf16[2,4000,256]{2,1,0:T(8,128)(2,1)}, bf16[4,128,256]{2,1,0:T(8,128)(2,1)}, bf16[4,512,256]{2,1,0:T(8,128)(2,1)}) async-done(((bf16[2,4000,256]{2,1,0:T(8,128)(2,1)}, bf16[4,128,256]{2,1,0:T(8,128)(2,1)}, bf16[4,512,256]{2,1,0:T(8,128)(2,1)}), (bf16[2,4000,256]{2,1,0:T(8,128)(2,1)}, bf16[4,128,256]{2,1,0:T(8,128)(2,1)}, ...) | async-done | bytes 5406736 | tf_op jit(solution)/shard_map/psum | solution.py:85
  135.5 11.6 %fusion.32 = bf16[2,1024,256]{1,2,0:T(8,128)(2,1)S(1)} fusion(bf16[2,4000,256]{2,1,0:T(8,128)(2,1)} %get-tuple-element.9, bf16[2,4000,1024]{2,1,0:T(8,128)(2,1)} %param.26), kind=kOutput, calls=%fused_computation.55 | convolution fusion | flops 4194828288 | bytes 21528576 | tf_op jit(solution)/shard_map/smc,smr->scr/dot_general | solution.py:87
  152.5 11.6 %copy.51 = bf16[10,1024,256]{2,0,1:T(8,128)(2,1)} copy(bf16[10,1024,256]{1,2,0:T(8,128)(2,1)} %pad_maximum_fusion.1) | data formatting | bytes 10485760
  164.1 9.2 %copy.53 = bf16[128,8,10,256]{3,1,2,0:T(8,128)(2,1)} copy(bf16[128,8,10,256]{3,2,1,0:T(8,128)(2,1)} %bitcast.110) | data formatting | bytes 10485760
  173.4 103.0 %reduce-scatter.7.cloned.1.call-done = bf16[128,2560]{1,0:T(8,128)(2,1)} async-done(((bf16[1024,2560]{1,0:T(8,128)(2,1)}), bf16[128,2560]{1,0:T(8,128)(2,1)}) %reduce-scatter.7.cloned.1.call-update) | async-done | bytes 655376
  281.4 137.8 %all-reduce.4.cloned.1.call-done = f32[10,256,256]{2,1,0:T(8,128)} async-done(((f32[10,256,256]{2,1,0:T(8,128)}), f32[10,256,256]{2,1,0:T(8,128)}) %all-reduce.4.cloned.1.call-update) | async-done | bytes 2621456 | tf_op jit(solution)/shard_map/psum | solution.py:92
  424.9 3.5 fusion.15
  428.3 3.3 fusion.14
  434.8 3.3 fusion.9
  440.8 3.3 fusion.10
  444.1 3.5 fusion.8
  453.5 3.3 convolution_convert_fusion.3
  456.8 84.8 %all-gather.4.cloned.1.call-done = bf16[10,1024,256]{2,1,0:T(8,128)(2,1)} async-done(((bf16[10,128,256]{2,1,0:T(8,128)(2,1)}), bf16[10,1024,256]{2,1,0:T(8,128)(2,1)}) %all-gather.4.cloned.1.call-update) | async-done | bytes 5242896 | tf_op jit(solution)/shard_map/all_gather | solution.py:94
  547.4 8.3 %convert_bitcast_fusion = bf16[4,2,1000,256]{3,2,0,1:T(8,128)(2,1)S(1)} fusion(bf16[2,4,1000,1024]{3,2,1,0:T(8,128)(2,1)} %bitcast.134, bf16[10,1024,256]{2,1,0:T(8,128)(2,1)} %all-gather.4.cloned.1.call-done), kind=kOutput, calls=%fused_computation.10 | convolution fusion | flops 4196352000 | bytes 21528576 | tf_op jit(solution)/shard_map/sjmc,scr->jsmr/dot_general | solution.py:105
  559.3 50.4 %reduce-scatter.5.cloned.1.call-done = bf16[1,2640,256]{2,1,0:T(8,128)(2,1)} async-done(((bf16[4,2640,256]{2,1,0:T(8,128)(2,1)}), bf16[1,2640,256]{2,1,0:T(8,128)(2,1)}) %reduce-scatter.5.cloned.1.call-update) | async-done | bytes 1351696 | tf_op jit(solution)/shard_map/reduce_scatter | solution.py:109
  615.2 3.5 divide_convert_fusion
  621.0 41.5 %all-gather.6.cloned.1.call-done = bf16[2703360]{0:T(1024)(128)(2,1)} async-done(((bf16[675840]{0:T(1024)(128)(2,1)}), bf16[2703360]{0:T(1024)(128)(2,1)}) %all-gather.6.cloned.1.call-update) | async-done | bytes 5406736 | tf_op jit(solution)/shard_map/all_gather | solution.py:115
  662.5 6.9 reshape.109
  676.2 4.7 broadcast_multiply_fusion
  680.9 7.2 fusion.1
  688.1 14.3 %convolution_multiply_fusion = f32[2,4,1000,1024]{3,2,1,0:T(8,128)} fusion(bf16[4,2,1000,256]{3,2,1,0:T(8,128)(2,1)S(1)} %bitcast.109, bf16[10,1024,256]{2,1,0:T(8,128)(2,1)} %all-gather.4.cloned.1.call-done), kind=kOutput, calls=%fused_computation.2 | convolution fusion | flops 4202496000 | bytes 37912576 | tf_op jit(solution)/shard_map/jsmr,scr->sjmc/dot_general | solution.py:120
  702.3 22.5 %fusion = bf16[2,4000,1024]{2,1,0:T(8,128)(2,1)} fusion(f32[2,4,1000,1024]{3,2,1,0:T(8,128)} %convolution_multiply_fusion, bf16[2,4000,1024]{2,1,0:T(8,128)(2,1)} %param.25), kind=kLoop, calls=%fused_computation.1 | loop fusion | flops 32768000 | bytes 65536000 | tf_op jit(solution)/shard_map/convert_element_type | solution.py:122
  (95 shorter events, 55.2 us)
Async XLA Ops:
  7.2 3.3 copy-start
  7.2 128.3 %all-reduce.6.cloned.1.call-start = ((), (), s32[]{:S(2)}) async-start(), calls=%async_computation.7 | async-start | bytes 10813440 | tf_op jit(solution)/shard_map/psum | solution.py:85
  10.4 4.5 copy-start.16
  27.0 249.4 %reduce-scatter.7.cloned.1.call-start = ((), (), s32[]{:S(2)}) async-start(), calls=%async_computation.6 | async-start | bytes 5898240
  135.5 11.6 %copy-start.5 = (bf16[4,128,1024]{2,1,0:T(8,128)(2,1)S(1)}, bf16[4,128,1024]{2,1,0:T(8,128)(2,1)}, u32[]{:S(2)}) copy-start(bf16[4,128,1024]{2,1,0:T(8,128)(2,1)} %param.21) | copy-start | bytes 3145732
  135.5 11.6 %copy-start.13 = (bf16[4,128,256]{2,1,0:T(8,128)(2,1)S(1)}, bf16[4,128,256]{2,1,0:T(8,128)(2,1)}, u32[]{:S(2)}) copy-start(bf16[4,128,256]{2,1,0:T(8,128)(2,1)} %get-tuple-element.10) | copy-start | bytes 786436
  135.5 12.4 %copy-start.3 = (bf16[4,512,1024]{2,1,0:T(8,128)(2,1)S(1)}, bf16[4,512,1024]{2,1,0:T(8,128)(2,1)}, u32[]{:S(2)}) copy-start(bf16[4,512,1024]{2,1,0:T(8,128)(2,1)} %param.16) | copy-start | bytes 12582916
  173.4 245.9 %all-reduce.4.cloned.1.call-start = ((), (), s32[]{:S(2)}) async-start(), calls=%async_computation.2 | async-start | bytes 5242880 | tf_op jit(solution)/shard_map/psum | solution.py:92
  280.8 260.9 %all-gather.4.cloned.1.call-start = ((), (), s32[]{:S(2)}) async-start(), calls=%async_computation.3 | async-start | bytes 5898240 | tf_op jit(solution)/shard_map/all_gather | solution.py:94
  419.3 2.5 copy-start.2
  456.8 152.9 %reduce-scatter.5.cloned.1.call-start = ((), (), s32[]{:S(2)}) async-start(), calls=%async_computation.4 | async-start | bytes 6758400 | tf_op jit(solution)/shard_map/reduce_scatter | solution.py:109
  541.7 2.8 copy-start.4
  558.8 51.7 %copy-start.14 = (f32[4,32,256]{2,1,0:T(8,128)S(1)}, f32[4,32,256]{2,1,0:T(8,128)}, u32[]{:S(2)}) copy-start(f32[4,32,256]{2,1,0:T(8,128)} %param.22) | copy-start | bytes 393220
  558.8 51.7 %copy-start.15 = (f32[4,32,256]{2,1,0:T(8,128)S(1)}, f32[4,32,256]{2,1,0:T(8,128)}, u32[]{:S(2)}) copy-start(f32[4,32,256]{2,1,0:T(8,128)} %param.23) | copy-start | bytes 393220
  558.8 53.5 %copy-start.11 = (f32[4,128,256]{2,1,0:T(8,128)S(1)}, f32[4,128,256]{2,1,0:T(8,128)}, u32[]{:S(2)}) copy-start(f32[4,128,256]{2,1,0:T(8,128)} %param.17) | copy-start | bytes 1572868
  558.8 53.5 %copy-start.12 = (f32[4,128,256]{2,1,0:T(8,128)S(1)}, f32[4,128,256]{2,1,0:T(8,128)}, u32[]{:S(2)}) copy-start(f32[4,128,256]{2,1,0:T(8,128)} %param.18) | copy-start | bytes 1572868
  558.9 103.6 %all-gather.6.cloned.1.call-start = ((), (), s32[]{:S(2)}) async-start(), calls=%async_computation.5 | async-start | bytes 6758400 | tf_op jit(solution)/shard_map/all_gather | solution.py:115
  612.3 2.3 copy-start.8
  612.3 2.9 copy-start.9
  669.4 2.3 slice-start.2
  669.4 4.1 slice-start.3
  671.7 2.0 slice-start.4
  676.2 4.7 copy-start.6
  702.3 22.5 %copy-start.1 = (bf16[4,1024,256]{2,1,0:T(8,128)(2,1)S(1)}, bf16[4,1024,256]{2,1,0:T(8,128)(2,1)}, u32[]{:S(2)}) copy-start(bf16[4,1024,256]{2,1,0:T(8,128)(2,1)} %param.19) | copy-start | bytes 6291460
  (5 other events, 6.7 us)
Sparse Core Ops, SparseCore 0:
  27.2 108.2 all-reduce.5
  173.5 102.8 reduce-scatter.6
  283.3 135.8 all-reduce.3
  456.9 84.6 all-gather.3
  559.0 50.6 reduce-scatter.4
  621.1 41.3 all-gather.5
where the time goes:
time: 737 us; the launch traced here: 732 us
  waiting for transfers between devices  526 us (71%)
  matrix products  103 us (14%)
  other arithmetic  45.9 us (6%)
  local copies, waits for them, and re-layouts  40.7 us (6%)
  between operations  14.7 us (2%)
    psum x1, waiting for transfers between devices, per_device(): grams = lax.psum(local_gram(backs), ('shard', 'tensor'))  138 us
    psum x1, waiting for transfers between devices, per_device(): sketches = lax.psum(tuple(sketch_terms), 'tensor')  108 us
    unnamed x7, waiting for transfers between devices  103 us
    all_gather x1, waiting for transfers between devices, per_device(): basis_all = lax.all_gather(rounded, 'shard', axis=1, tiled=True)  84.8 us
    reduce_scatter x1, waiting for transfers between devices, per_device(): lax.psum_scatter(proj_all, 'tensor', scatter_dimension=0, tiled=True)  50.4 us
    all_gather x1, waiting for transfers between devices, per_device(): dir_gathered = lax.all_gather(dir_all, 'tensor', axis=0, tiled=False)  41.5 us
    convert_element_type x3, other arithmetic, per_device(): (0.99 * weight.astype(jnp.float32) - 2.0 * update).astype(jnp.bfloat16)  31.1 us
    unnamed x48, local copies, waits for them, and re-layouts  28.2 us
  transfers between devices with their start and end apart: 6, of which 6 were waited for; matrix products, arithmetic and copies ran while one was open for 0% of the time, Pallas kernels for 0%

commit v1 on v0

--- a/solution.py
+++ b/solution.py
@@ -89,7 +89,7 @@
     ]
     back_all = jnp.concatenate(back_terms, axis=0).astype(jnp.bfloat16)
     backs = lax.psum_scatter(back_all, "shard", scatter_dimension=1, tiled=True).astype(jnp.float32)
-    grams = lax.psum(local_gram(backs), ("shard", "tensor"))
+    grams = lax.psum(lax.psum(local_gram(backs), "tensor"), "shard")
     rounded = polish_small(backs, grams).astype(jnp.bfloat16)
     basis_all = lax.all_gather(rounded, "shard", axis=1, tiled=True)
     bases = []

time: 737 us -> 779 us (1.057)
  waiting for transfers between devices: 526 us -> 567 us
    psum x1 -> x2, waiting for transfers between devices: 138 us -> 179 us  [per_device(): grams = lax.psum(lax.psum(local_gram(backs), 'tensor'), 'shard')]
    unnamed x7 -> x8, waiting for transfers between devices: 103 us -> 103 us
  transfers between devices with their start and end apart: 6 -> 7, of which waited for: 6 -> 7; matrix products, arithmetic and copies ran while one was open for 0% -> 0% of each run, Pallas kernels for 0% -> 0%
where the time goes in v1:
time: 779 us; the launch traced here: 774 us
  waiting for transfers between devices  567 us (73%)
  matrix products  103 us (13%)
  other arithmetic  45.9 us (6%)
  local copies, waits for them, and re-layouts  40.7 us (5%)
  between operations  14.7 us (2%)
    psum x2, waiting for transfers between devices, per_device(): grams = lax.psum(lax.psum(local_gram(backs), 'tensor'), 'shard')  179 us
    psum x1, waiting for transfers between devices, per_device(): sketches = lax.psum(tuple(sketch_terms), 'tensor')  108 us
    unnamed x8, waiting for transfers between devices  103 us
    all_gather x1, waiting for transfers between devices, per_device(): basis_all = lax.all_gather(rounded, 'shard', axis=1, tiled=True)  85.4 us
    reduce_scatter x1, waiting for transfers between devices, per_device(): lax.psum_scatter(proj_all, 'tensor', scatter_dimension=0, tiled=True)  50.4 us
    all_gather x1, waiting for transfers between devices, per_device(): dir_gathered = lax.all_gather(dir_all, 'tensor', axis=0, tiled=False)  41.5 us
    convert_element_type x3, other arithmetic, per_device(): (0.99 * weight.astype(jnp.float32) - 2.0 * update).astype(jnp.bfloat16)  31.1 us
    unnamed x48, local copies, waits for them, and re-layouts  28.2 us
  transfers between devices with their start and end apart: 7, of which 7 were waited for; matrix products, arithmetic and copies ran while one was open for 0% of the time, Pallas kernels for 0%

profile of v1, /device:TPU:0, one launch (start us, length us, event | category | flops | bytes accessed | tf_op | source)
XLA Modules:
  0.0 773.7 jit_solution(6559998780811933607)
XLA Ops:
  10.4 4.5 convolution_convert_fusion.2
  14.9 12.1 %convolution_convert_fusion = bf16[2,4000,256]{2,1,0:T(8,128)(2,1)} fusion(bf16[2,4000,1024]{2,1,0:T(8,128)(2,1)} %param.26, bf16[2,1024,256]{2,1,0:T(8,128)(2,1)S(1)} %copy-done.16), kind=kOutput, calls=%fused_computation.5 | convolution fusion | flops 4196352000 | bytes 21528576 | tf_op jit(solution)/shard_map/smc,scr->smr/dot_general | solution.py:80
  27.4 108.1 %all-reduce.9.cloned.1.call-done = (bf16[2,4000,256]{2,1,0:T(8,128)(2,1)}, bf16[4,128,256]{2,1,0:T(8,128)(2,1)}, bf16[4,512,256]{2,1,0:T(8,128)(2,1)}) async-done(((bf16[2,4000,256]{2,1,0:T(8,128)(2,1)}, bf16[4,128,256]{2,1,0:T(8,128)(2,1)}, bf16[4,512,256]{2,1,0:T(8,128)(2,1)}), (bf16[2,4000,256]{2,1,0:T(8,128)(2,1)}, bf16[4,128,256]{2,1,0:T(8,128)(2,1)}, ...) | async-done | bytes 5406736 | tf_op jit(solution)/shard_map/psum | solution.py:85
  135.5 11.6 %fusion.32 = bf16[2,1024,256]{1,2,0:T(8,128)(2,1)S(1)} fusion(bf16[2,4000,256]{2,1,0:T(8,128)(2,1)} %get-tuple-element.9, bf16[2,4000,1024]{2,1,0:T(8,128)(2,1)} %param.26), kind=kOutput, calls=%fused_computation.55 | convolution fusion | flops 4194828288 | bytes 21528576 | tf_op jit(solution)/shard_map/smc,smr->scr/dot_general | solution.py:87
  152.5 11.6 %copy.51 = bf16[10,1024,256]{2,0,1:T(8,128)(2,1)} copy(bf16[10,1024,256]{1,2,0:T(8,128)(2,1)} %pad_maximum_fusion.1) | data formatting | bytes 10485760
  164.1 9.2 %copy.53 = bf16[128,8,10,256]{3,1,2,0:T(8,128)(2,1)} copy(bf16[128,8,10,256]{3,2,1,0:T(8,128)(2,1)} %bitcast.110) | data formatting | bytes 10485760
  173.4 103.0 %reduce-scatter.7.cloned.1.call-done = bf16[128,2560]{1,0:T(8,128)(2,1)} async-done(((bf16[1024,2560]{1,0:T(8,128)(2,1)}), bf16[128,2560]{1,0:T(8,128)(2,1)}) %reduce-scatter.7.cloned.1.call-update) | async-done | bytes 655376
  280.8 59.8 %all-reduce.5.cloned.1.call-done = f32[10,256,256]{2,1,0:T(8,128)} async-done(((f32[10,256,256]{2,1,0:T(8,128)}), f32[10,256,256]{2,1,0:T(8,128)}) %all-reduce.5.cloned.1.call-update) | async-done | bytes 2621456 | tf_op jit(solution)/shard_map/psum | solution.py:92
  341.3 119.2 %all-reduce.7.cloned.1.call-done = f32[10,256,256]{2,1,0:T(8,128)} async-done(((f32[10,256,256]{2,1,0:T(8,128)}), f32[10,256,256]{2,1,0:T(8,128)}) %all-reduce.7.cloned.1.call-update) | async-done | bytes 2621456 | tf_op jit(solution)/shard_map/psum | solution.py:92
  466.1 3.5 fusion.15
  469.5 3.3 fusion.14
  476.0 3.3 fusion.9
  485.3 3.5 fusion.8
  494.7 3.3 convolution_convert_fusion.3
  498.1 85.4 %all-gather.4.cloned.1.call-done = bf16[10,1024,256]{2,1,0:T(8,128)(2,1)} async-done(((bf16[10,128,256]{2,1,0:T(8,128)(2,1)}), bf16[10,1024,256]{2,1,0:T(8,128)(2,1)}) %all-gather.4.cloned.1.call-update) | async-done | bytes 5242896 | tf_op jit(solution)/shard_map/all_gather | solution.py:94
  589.3 8.3 %convert_bitcast_fusion = bf16[4,2,1000,256]{3,2,0,1:T(8,128)(2,1)S(1)} fusion(bf16[2,4,1000,1024]{3,2,1,0:T(8,128)(2,1)} %bitcast.134, bf16[10,1024,256]{2,1,0:T(8,128)(2,1)} %all-gather.4.cloned.1.call-done), kind=kOutput, calls=%fused_computation.10 | convolution fusion | flops 4196352000 | bytes 21528576 | tf_op jit(solution)/shard_map/sjmc,scr->jsmr/dot_general | solution.py:105
  601.1 50.4 %reduce-scatter.5.cloned.1.call-done = bf16[1,2640,256]{2,1,0:T(8,128)(2,1)} async-done(((bf16[4,2640,256]{2,1,0:T(8,128)(2,1)}), bf16[1,2640,256]{2,1,0:T(8,128)(2,1)}) %reduce-scatter.5.cloned.1.call-update) | async-done | bytes 1351696 | tf_op jit(solution)/shard_map/reduce_scatter | solution.py:109
  657.0 3.5 divide_convert_fusion
  662.8 41.5 %all-gather.6.cloned.1.call-done = bf16[2703360]{0:T(1024)(128)(2,1)} async-done(((bf16[675840]{0:T(1024)(128)(2,1)}), bf16[2703360]{0:T(1024)(128)(2,1)}) %all-gather.6.cloned.1.call-update) | async-done | bytes 5406736 | tf_op jit(solution)/shard_map/all_gather | solution.py:115
  704.3 6.9 reshape.109
  718.0 4.7 broadcast_multiply_fusion
  722.7 7.2 fusion.1
  729.9 14.3 %convolution_multiply_fusion = f32[2,4,1000,1024]{3,2,1,0:T(8,128)} fusion(bf16[4,2,1000,256]{3,2,1,0:T(8,128)(2,1)S(1)} %bitcast.109, bf16[10,1024,256]{2,1,0:T(8,128)(2,1)} %all-gather.4.cloned.1.call-done), kind=kOutput, calls=%fused_computation.2 | convolution fusion | flops 4202496000 | bytes 37912576 | tf_op jit(solution)/shard_map/jsmr,scr->sjmc/dot_general | solution.py:120
  744.2 22.5 %fusion = bf16[2,4000,1024]{2,1,0:T(8,128)(2,1)} fusion(f32[2,4,1000,1024]{3,2,1,0:T(8,128)} %convolution_multiply_fusion, bf16[2,4000,1024]{2,1,0:T(8,128)(2,1)} %param.25), kind=kLoop, calls=%fused_computation.1 | loop fusion | flops 32768000 | bytes 65536000 | tf_op jit(solution)/shard_map/convert_element_type | solution.py:122
  (98 shorter events, 58.6 us)
Async XLA Ops:
  7.2 3.3 copy-start
  7.2 128.3 %all-reduce.9.cloned.1.call-start = ((), (), s32[]{:S(2)}) async-start(), calls=%async_computation.8 | async-start | bytes 10813440 | tf_op jit(solution)/shard_map/psum | solution.py:85
  10.4 4.5 copy-start.16
  27.0 249.4 %reduce-scatter.7.cloned.1.call-start = ((), (), s32[]{:S(2)}) async-start(), calls=%async_computation.7 | async-start | bytes 5898240
  135.5 11.6 %copy-start.5 = (bf16[4,128,1024]{2,1,0:T(8,128)(2,1)S(1)}, bf16[4,128,1024]{2,1,0:T(8,128)(2,1)}, u32[]{:S(2)}) copy-start(bf16[4,128,1024]{2,1,0:T(8,128)(2,1)} %param.21) | copy-start | bytes 3145732
  135.5 11.6 %copy-start.13 = (bf16[4,128,256]{2,1,0:T(8,128)(2,1)S(1)}, bf16[4,128,256]{2,1,0:T(8,128)(2,1)}, u32[]{:S(2)}) copy-start(bf16[4,128,256]{2,1,0:T(8,128)(2,1)} %get-tuple-element.10) | copy-start | bytes 786436
  135.5 12.4 %copy-start.3 = (bf16[4,512,1024]{2,1,0:T(8,128)(2,1)S(1)}, bf16[4,512,1024]{2,1,0:T(8,128)(2,1)}, u32[]{:S(2)}) copy-start(bf16[4,512,1024]{2,1,0:T(8,128)(2,1)} %param.16) | copy-start | bytes 12582916
  173.4 167.2 %all-reduce.5.cloned.1.call-start = ((), (), s32[]{:S(2)}) async-start(), calls=%async_computation.2 | async-start | bytes 5242880 | tf_op jit(solution)/shard_map/psum | solution.py:92
  280.8 179.7 %all-reduce.7.cloned.1.call-start = ((), (), s32[]{:S(2)}) async-start(), calls=%async_computation.3 | async-start | bytes 5242880 | tf_op jit(solution)/shard_map/psum | solution.py:92
  340.6 242.9 %all-gather.4.cloned.1.call-start = ((), (), s32[]{:S(2)}) async-start(), calls=%async_computation.4 | async-start | bytes 5898240 | tf_op jit(solution)/shard_map/all_gather | solution.py:94
  460.5 2.5 copy-start.2
  498.0 153.5 %reduce-scatter.5.cloned.1.call-start = ((), (), s32[]{:S(2)}) async-start(), calls=%async_computation.5 | async-start | bytes 6758400 | tf_op jit(solution)/shard_map/reduce_scatter | solution.py:109
  583.5 2.8 copy-start.4
  600.6 51.7 %copy-start.14 = (f32[4,32,256]{2,1,0:T(8,128)S(1)}, f32[4,32,256]{2,1,0:T(8,128)}, u32[]{:S(2)}) copy-start(f32[4,32,256]{2,1,0:T(8,128)} %param.22) | copy-start | bytes 393220
  600.6 51.7 %copy-start.15 = (f32[4,32,256]{2,1,0:T(8,128)S(1)}, f32[4,32,256]{2,1,0:T(8,128)}, u32[]{:S(2)}) copy-start(f32[4,32,256]{2,1,0:T(8,128)} %param.23) | copy-start | bytes 393220
  600.6 53.5 %copy-start.11 = (f32[4,128,256]{2,1,0:T(8,128)S(1)}, f32[4,128,256]{2,1,0:T(8,128)}, u32[]{:S(2)}) copy-start(f32[4,128,256]{2,1,0:T(8,128)} %param.17) | copy-start | bytes 1572868
  600.6 53.5 %copy-start.12 = (f32[4,128,256]{2,1,0:T(8,128)S(1)}, f32[4,128,256]{2,1,0:T(8,128)}, u32[]{:S(2)}) copy-start(f32[4,128,256]{2,1,0:T(8,128)} %param.18) | copy-start | bytes 1572868
  600.7 103.6 %all-gather.6.cloned.1.call-start = ((), (), s32[]{:S(2)}) async-start(), calls=%async_computation.6 | async-start | bytes 6758400 | tf_op jit(solution)/shard_map/all_gather | solution.py:115
  654.1 2.3 copy-start.8
  654.2 2.9 copy-start.9
  711.3 2.3 slice-start.2
  711.3 4.1 slice-start.3
  718.0 4.7 copy-start.6
  744.2 22.5 %copy-start.1 = (bf16[4,1024,256]{2,1,0:T(8,128)(2,1)S(1)}, bf16[4,1024,256]{2,1,0:T(8,128)(2,1)}, u32[]{:S(2)}) copy-start(bf16[4,1024,256]{2,1,0:T(8,128)(2,1)} %param.19) | copy-start | bytes 6291460
  (6 other events, 8.7 us)
Sparse Core Ops, SparseCore 0:
  27.2 108.2 all-reduce.8
  173.5 102.8 reduce-scatter.6
  280.9 59.6 all-reduce.4
  344.5 115.8 all-reduce.6
  498.1 85.2 all-gather.3
  600.8 50.6 reduce-scatter.4
  662.9 41.3 all-gather.5
